TPU v7x, 256 devices: a whole 4x4x8 slice. The times are simulated.
256 devices in a mesh: req: 32 (over z, x_hi, core), mlp: 8 (over x_lo, y).
Axes of the slice: x: 4 (x_hi: 2, x_lo: 2; x = x_hi * 2 + x_lo), y: 4, z: 8, core: 2. Of those that a mesh axis runs over, the one named last changes fastest.
Arguments:
- residual_in: bfloat16 [1024, 2560], P('req'), may hold values from -6 to 6
- queries: bfloat16 [1024, 2560], P('req', 'mlp')
- fresh_rotated_keys: bfloat16 [1024, 640], P('req', 'mlp'), may hold values from -6 to 6
- fresh_value_rows: bfloat16 [1024, 640], P('req', 'mlp'), may hold values from -6 to 6
- shared_prefix_keys: bfloat16 [32, 16384, 640], P(None, 'req', 'mlp'), may hold values from -6 to 6
- shared_prefix_values: bfloat16 [32, 16384, 640], P(None, 'req', 'mlp'), may hold values from -6 to 6
- sample_tail_keys: bfloat16 [32, 16, 128, 640], P('req', None, None, 'mlp'), may hold values from -6 to 6
- sample_tail_values: bfloat16 [32, 16, 128, 640], P('req', None, None, 'mlp'), may hold values from -6 to 6
- prompt_prefix_length: int32 [32], replicated, may hold values from 1 to 16384, as said below
- sample_tail_length: int32 [32, 16], P('req'), may hold values from 0 to 128, as said below
- out_weight: bfloat16 [2560, 2560], P('mlp'), may hold values from -0.125 to 0.125
- gate_weight: bfloat16 [2560, 4096], P(None, 'mlp'), may hold values from -0.125 to 0.125
- up_weight: bfloat16 [2560, 4096], P(None, 'mlp'), may hold values from -0.125 to 0.125
- down_weight: bfloat16 [4096, 2560], P('mlp'), may hold values from -0.09375 to 0.09375
- mlp_gain: float32 [2560], replicated, may hold values from 0.1 to 1.9
- final_gain: float32 [2560], replicated, may hold values from 0.1 to 1.9
- score_weight: float32 [2560], replicated, may hold values from -0.125 to 0.125
Outputs:
- layer_out: bfloat16 [1024, 2560], P('req', 'mlp')
- score: float32 [1024], P('req')
Inputs may be any that keep to these rules, and one draw needn't show every extreme that they name: `prompt_prefix_length`: one prompt in every draw has the full prefix length 16384. `sample_tail_length`: one sample in every draw has the full tail length 128.
All inputs are finite; a program needn't handle non-finite values.
Results may differ from a plain program's by a relative error of at most 0.02.
Values may be sent and summed in bfloat16 or wider, within the bound.
No kernel may reach another device: no remote copies, remote signals or barrier semaphores. Data moves between devices by JAX's collectives and lax.ppermute only.
A program may use at most 128 MiB of HBM per device.

v0:
```python
import jax
import jax.numpy as jnp
from jax import lax
from jax.sharding import PartitionSpec as P

D = 2560
QUERY_HEADS = 32
KEY_VALUE_HEADS = 8
HEAD_SIZE = 80
SAMPLE_COUNT = 16
DECODE_TOKENS = 2
TAIL_LENGTH = 128


def rms_scale(total_sq, width):
    return lax.rsqrt(total_sq / width + 1e-05)


def on_device(
    residual_in,
    queries,
    fresh_rotated_keys,
    fresh_value_rows,
    shared_prefix_keys,
    shared_prefix_values,
    sample_tail_keys,
    sample_tail_values,
    prompt_prefix_length,
    sample_tail_length,
    out_weight,
    gate_weight,
    up_weight,
    down_weight,
    mlp_gain,
    final_gain,
    score_weight,
):
    query_groups = QUERY_HEADS // KEY_VALUE_HEADS
    inv_root = HEAD_SIZE ** (-0.5)
    kv_local = fresh_rotated_keys.shape[1] // HEAD_SIZE
    prompts = shared_prefix_keys.shape[0]
    piece_len = shared_prefix_keys.shape[1]
    req_index = lax.axis_index("req")
    low = jnp.float32(-1e30)
    gathered = lax.all_gather(queries, "req", axis=0, tiled=True)
    query_all = gathered.reshape(
        prompts, SAMPLE_COUNT, DECODE_TOKENS, kv_local, query_groups, HEAD_SIZE
    )
    prefix_key_block = shared_prefix_keys.reshape(prompts, piece_len, kv_local, HEAD_SIZE)
    prefix_value_block = shared_prefix_values.reshape(prompts, piece_len, kv_local, HEAD_SIZE)
    score_pre = (
        jnp.einsum(
            "psjkgh,plkh->pksjgl", query_all, prefix_key_block, preferred_element_type=jnp.float32
        )
        * inv_root
    )
    key_place = req_index * piece_len + jnp.arange(piece_len)
    valid = (key_place[None, :] < prompt_prefix_length[:, None])[:, None, None, None, None, :]
    piece_top = jnp.max(jnp.where(valid, score_pre, low), -1)
    piece_w = jnp.where(valid, jnp.exp(score_pre - piece_top[..., None]), 0.0)
    piece_sum = jnp.sum(piece_w, -1)
    piece_out = jnp.einsum(
        "pksjgl,plkh->pksjgh",
        piece_w.astype(jnp.bfloat16),
        prefix_value_block,
        preferred_element_type=jnp.float32,
    )
    source_out, source_top, source_sum = (
        lax.all_to_all(piece_out, "req", split_axis=0, concat_axis=0, tiled=True),
        lax.all_to_all(piece_top, "req", split_axis=0, concat_axis=0, tiled=True),
        lax.all_to_all(piece_sum, "req", split_axis=0, concat_axis=0, tiled=True),
    )
    query_own = queries.reshape(SAMPLE_COUNT, DECODE_TOKENS, kv_local, query_groups, HEAD_SIZE)
    tail_key_block = sample_tail_keys.reshape(SAMPLE_COUNT, TAIL_LENGTH, kv_local, HEAD_SIZE)
    tail_value_block = sample_tail_values.reshape(SAMPLE_COUNT, TAIL_LENGTH, kv_local, HEAD_SIZE)
    fresh_k = fresh_rotated_keys.reshape(SAMPLE_COUNT, DECODE_TOKENS, kv_local, HEAD_SIZE)
    fresh_v = fresh_value_rows.reshape(SAMPLE_COUNT, DECODE_TOKENS, kv_local, HEAD_SIZE)
    score_tail = (
        jnp.einsum(
            "sjkgh,stkh->ksjgt", query_own, tail_key_block, preferred_element_type=jnp.float32
        )
        * inv_root
    )
    score_new = (
        jnp.einsum("sjkgh,sikh->ksjgi", query_own, fresh_k, preferred_element_type=jnp.float32)
        * inv_root
    )
    mask_tail = (jnp.arange(TAIL_LENGTH)[None, :] < sample_tail_length[0][:, None])[
        None, :, None, None, :
    ]
    causal = (jnp.arange(DECODE_TOKENS)[None, :] <= jnp.arange(DECODE_TOKENS)[:, None])[
        None, None, :, None, :
    ]
    local_top = jnp.maximum(
        jnp.max(jnp.where(mask_tail, score_tail, low), -1),
        jnp.max(jnp.where(causal, score_new, low), -1),
    )
    w_tail = jnp.where(mask_tail, jnp.exp(score_tail - local_top[..., None]), 0.0)
    w_new = jnp.where(causal, jnp.exp(score_new - local_top[..., None]), 0.0)
    local_sum = jnp.sum(w_tail, -1) + jnp.sum(w_new, -1)
    local_out = jnp.einsum(
        "ksjgt,stkh->ksjgh",
        w_tail.astype(jnp.bfloat16),
        tail_value_block,
        preferred_element_type=jnp.float32,
    )
    local_out = local_out + jnp.einsum(
        "ksjgi,sikh->ksjgh", w_new.astype(jnp.bfloat16), fresh_v, preferred_element_type=jnp.float32
    )
    overall = jnp.maximum(jnp.max(source_top, 0), local_top)
    source_w = jnp.exp(source_top - overall[None])
    local_w = jnp.exp(local_top - overall)
    numer = jnp.sum(source_w[..., None] * source_out, 0) + local_w[..., None] * local_out
    denom = jnp.sum(source_w * source_sum, 0) + local_w * local_sum
    attention_layer = (numer / denom[..., None]).astype(jnp.bfloat16)
    attention_layer = jnp.transpose(attention_layer, (1, 2, 0, 3, 4)).reshape(
        SAMPLE_COUNT * DECODE_TOKENS, kv_local * query_groups * HEAD_SIZE
    )
    projected = jnp.dot(attention_layer, out_weight, preferred_element_type=jnp.float32)
    mlp_count = lax.axis_size("mlp")
    mlp_index = lax.axis_index("mlp")
    share = D // mlp_count
    mid = residual_in.astype(jnp.float32) + lax.psum(projected.astype(jnp.bfloat16), "mlp").astype(
        jnp.float32
    )
    normed = (mid * rms_scale(jnp.sum(mid * mid, -1, keepdims=True), D) * mlp_gain).astype(
        jnp.bfloat16
    )
    gate = jnp.dot(normed, gate_weight, preferred_element_type=jnp.float32)
    upper = jnp.dot(normed, up_weight, preferred_element_type=jnp.float32)
    hidden = (jax.nn.silu(gate) * upper).astype(jnp.bfloat16)
    stream = mid + lax.psum(
        jnp.dot(hidden, down_weight, preferred_element_type=jnp.float32).astype(jnp.bfloat16), "mlp"
    ).astype(jnp.float32)
    score = jnp.sum(
        stream
        * rms_scale(jnp.sum(stream * stream, -1, keepdims=True), D)
        * final_gain
        * score_weight,
        -1,
    )
    layer_out = lax.dynamic_slice_in_dim(stream, mlp_index * share, share, 1).astype(jnp.bfloat16)
    return (layer_out, score)


def solution(mesh):
    placed = (
        P("req", None),
        P("req", "mlp"),
        P("req", "mlp"),
        P("req", "mlp"),
        P(None, "req", "mlp"),
        P(None, "req", "mlp"),
        P("req", None, None, "mlp"),
        P("req", None, None, "mlp"),
        P(),
        P("req", None),
        P("mlp", None),
        P(None, "mlp"),
        P(None, "mlp"),
        P("mlp", None),
        P(),
        P(),
        P(),
    )
    return jax.shard_map(
        on_device,
        mesh=mesh,
        in_specs=placed,
        out_specs=(P("req", "mlp"), P("req")),
        check_vma=False,
    )
```

profile of v0, /device:TPU:6, one launch (start us, length us, event | category | flops | bytes accessed | tf_op | source)
XLA Modules:
  0.0 322.3 jit_solution(5369909995095081894)
XLA Ops:
  7.2 0.0 copy-start
  7.2 43.4 %all_gather.3 = bf16[1024,320]{1,0:T(8,128)(2,1)S(1)} all-gather(bf16[32,320]{1,0:T(8,128)(2,1)} %param.18), channel_id=1, replica_groups=mesh['req'=32,'mlp'=8] {'req'}, dimensions={0}, use_global_device_ids=true | all-gather | bytes 675840 | tf_op jit(solution)/shard_map/all_gather | solution.py:45
  50.6 1.6 reshape.254
  52.3 0.1 broadcast_compare_fusion
  52.4 2.8 select_reduce_fusion
  55.2 0.0 copy-start.1
  55.2 2.3 fusion
  57.4 0.9 copy-done.1
  58.4 0.7 reshape.268
  59.1 8.4 %all-to-all-start.2 = ((f32[32,1,128]{2,1,0:T(1,128)}), f32[32,1,128]{2,1,0:T(1,128)S(1)}, u32[]{:S(2)}, u32[]{:S(2)}) async-start(f32[32,1,128]{2,1,0:T(1,128)} %reshape.268), calls=%async_computation.2 | async-start | bytes 32768 | tf_op jit(solution)/shard_map/all_to_all | solution.py:71
  67.6 0.7 reshape.266
  68.3 6.4 %all-to-all-done.2 = f32[32,1,128]{2,1,0:T(1,128)S(1)} async-done(((f32[32,1,128]{2,1,0:T(1,128)}), f32[32,1,128]{2,1,0:T(1,128)S(1)}, u32[]{:S(2)}, u32[]{:S(2)}) %all-to-all-start.2) | async-done | bytes 16416 | tf_op jit(solution)/shard_map/all_to_all | solution.py:71
  74.7 6.3 %all-to-all-start = ((f32[32,1,128]{2,1,0:T(1,128)}), f32[32,1,128]{2,1,0:T(1,128)S(1)}, u32[]{:S(2)}, u32[]{:S(2)}) async-start(f32[32,1,128]{2,1,0:T(1,128)} %reshape.266), calls=%async_computation | async-start | bytes 32768 | tf_op jit(solution)/shard_map/all_to_all | solution.py:70
  81.0 7.2 %fusion.11 = f32[32,1,16,2,4,80]{5,2,4,3,1,0:T(8,128)} fusion(bf16[32,512,80]{1,2,0:T(8,128)(2,1)} %param.22, f32[32,16,2,4,512]{4,1,3,2,0:T(8,128)} %copy-done.1, f32[32,16,2,4]{1,3,2,0:T(4,128)S(1)} %get-tuple-element.8, pred[32,512]{1,0:T(8,128)(4,1)S(1)} %broadcast_compare_fusion), kind=kOutput, calls=%fused_computation.15 | convolution fusion | flops 343932928 | bytes 12353536 | tf_op jit(solution)/shard_map/pksjgl,plkh->pksjgh/dot_general | solution.py:62
  88.3 0.0 copy-start.11
  88.3 0.0 all-to-all-done
  88.3 10.1 %all-to-all-start.1 = ((f32[32,1,16,2,4,80]{5,2,4,3,1,0:T(8,128)}), f32[32,1,16,2,4,80]{5,2,4,3,1,0:T(8,128)}, u32[]{:S(2)}, u32[]{:S(2)}) async-start(f32[32,1,16,2,4,80]{5,2,4,3,1,0:T(8,128)} %fusion.11), calls=%async_computation.1 | async-start | bytes 4194304 | tf_op jit(solution)/shard_map/all_to_all | solution.py:69
  98.4 0.0 all-reduce.3.cloned.1.call-start
  98.4 0.1 reshape.255
  98.5 0.0 copy-done.12
  98.5 0.4 select_reduce_fusion.2
  99.0 0.0 copy-start.13
  99.0 0.1 copy.35
  99.1 0.1 iota_compare_fusion
  99.2 0.3 select_reduce_fusion.1
  99.4 0.1 copy.34
  99.5 0.5 broadcast.104
  100.1 0.7 reduce.15
  100.7 0.1 reshape.267
  100.9 0.1 bitcast_reduce_fusion.2
  100.9 0.1 copy.39
  101.0 0.1 fusion.39
  101.2 0.1 copy.44
  101.3 0.2 fusion.31
  101.5 0.1 copy.43
  101.6 0.7 reduce.16
  102.3 0.1 reshape.269
  102.4 0.1 bitcast_reduce_fusion.1
  102.5 0.1 copy.45
  102.6 0.1 copy.38
  102.8 0.3 fusion.22
  103.1 45.6 %all-to-all-done.1 = f32[32,1,16,2,4,80]{5,2,4,3,1,0:T(8,128)} async-done(((f32[32,1,16,2,4,80]{5,2,4,3,1,0:T(8,128)}), f32[32,1,16,2,4,80]{5,2,4,3,1,0:T(8,128)}, u32[]{:S(2)}, u32[]{:S(2)}) %all-to-all-start.1) | async-done | bytes 1310752 | tf_op jit(solution)/shard_map/all_to_all | solution.py:69
  148.7 1.9 bitcast_reduce_fusion
  150.6 0.0 copy-start.2
  150.6 0.0 copy-start.6
  150.6 0.3 fusion.19
  150.9 0.1 reshape_transpose.3
  151.0 2.5 convolution_convert_fusion.1
  153.5 0.0 all-reduce.3.cloned.1.call-update
  153.5 0.0 all-reduce.5.cloned.1.call-start
  153.6 74.1 %all-reduce.3.cloned.1.call-done = bf16[32,2560]{1,0:T(8,128)(2,1)} async-done(((bf16[32,2560]{1,0:T(8,128)(2,1)}), bf16[32,2560]{1,0:T(8,128)(2,1)}) %all-reduce.3.cloned.1.call-update) | async-done | bytes 163856 | tf_op jit(solution)/shard_map/psum | solution.py:123
  227.7 0.0 copy-done.2
  227.7 1.1 multiply_reduce_fusion.2
  228.9 2.4 fusion.45
  231.3 0.0 copy-done.3
  231.3 0.0 copy-start.7
  231.3 0.0 copy-start.8
  231.3 4.3 %convolution_convert_fusion = bf16[32,2560]{1,0:T(8,128)(2,1)} fusion(bf16[512,2560]{1,0:T(8,128)(2,1)} %param.30, bf16[2560,512]{1,0:T(8,128)(2,1)} %param.29, f32[32,512]{1,0:T(8,128)S(1)} %fusion.45, bf16[32,2560]{1,0:T(8,128)(2,1)S(1)} %copy-done.3, bf16[32,2560]{1,0:T(8,128)(2,1)S(1)} %copy-done.2, f32[2560]{0:T(1024)S(1)} %copy-done.6, ...), kind=kOutput, calls=%fused_computation.9 | convolution fusion | flops 168443904 | bytes 5810304 | tf_op jit(solution)/shard_map/dot_general | solution.py:133
  235.7 0.0 all-reduce.5.cloned.1.call-update
  235.7 77.2 %all-reduce.5.cloned.1.call-done = bf16[32,2560]{1,0:T(8,128)(2,1)} async-done(((bf16[32,2560]{1,0:T(8,128)(2,1)}), bf16[32,2560]{1,0:T(8,128)(2,1)}) %all-reduce.5.cloned.1.call-update) | async-done | bytes 163856 | tf_op jit(solution)/shard_map/psum | solution.py:132
  312.9 1.1 multiply_reduce_fusion.1
  314.0 0.7 dynamic-slice_convert_fusion
  314.7 0.0 copy-done.7
  314.7 0.7 multiply_reduce_fusion
  (24 shorter events, 0.1 us)
Async XLA Ops:
  7.2 45.2 %copy-start = (bf16[32,512,80]{1,2,0:T(8,128)(2,1)S(1)}, bf16[32,512,80]{1,2,0:T(8,128)(2,1)}, u32[]{:S(2)}) copy-start(bf16[32,512,80]{1,2,0:T(8,128)(2,1)} %param.21) | copy-start | bytes 7864324
  7.2 45.1 %copy-start.9 = (s32[32]{0:T(128)S(1)}, s32[32]{0:T(128)}, u32[]{:S(2)}) copy-start(s32[32]{0:T(128)} %param.25) | copy-start | bytes 388
  55.2 3.2 copy-start.1
  59.1 15.6 %all-to-all-start.2 = ((f32[32,1,128]{2,1,0:T(1,128)}), f32[32,1,128]{2,1,0:T(1,128)S(1)}, u32[]{:S(2)}, u32[]{:S(2)}) async-start(f32[32,1,128]{2,1,0:T(1,128)} %reshape.268), calls=%async_computation.2 | async-start | bytes 32768 | tf_op jit(solution)/shard_map/all_to_all | solution.py:71
  74.7 13.6 %all-to-all-start = ((f32[32,1,128]{2,1,0:T(1,128)}), f32[32,1,128]{2,1,0:T(1,128)S(1)}, u32[]{:S(2)}, u32[]{:S(2)}) async-start(f32[32,1,128]{2,1,0:T(1,128)} %reshape.266), calls=%async_computation | async-start | bytes 32768 | tf_op jit(solution)/shard_map/all_to_all | solution.py:70
  88.3 10.2 %copy-start.5 = (bf16[32,320]{1,0:T(8,128)(2,1)S(1)}, bf16[32,320]{1,0:T(8,128)(2,1)}, u32[]{:S(2)}) copy-start(bf16[32,320]{1,0:T(8,128)(2,1)} %param.18) | copy-start | bytes 61444
  88.3 10.3 %copy-start.12 = (bf16[32,80]{1,0:T(8,128)(2,1)S(1)}, bf16[32,80]{1,0:T(8,128)(2,1)}, u32[]{:S(2)}) copy-start(bf16[32,80]{1,0:T(8,128)(2,1)} %param.19) | copy-start | bytes 15364
  88.3 10.8 %copy-start.10 = (s32[1,16]{1,0:T(1,128)S(1)}, s32[1,16]{1,0:T(1,128)}, u32[]{:S(2)}) copy-start(s32[1,16]{1,0:T(1,128)} %param.26) | copy-start | bytes 196
  88.3 10.9 %copy-start.4 = (bf16[1,16,128,80]{2,3,1,0:T(8,128)(2,1)S(1)}, bf16[1,16,128,80]{2,3,1,0:T(8,128)(2,1)}, u32[]{:S(2)}) copy-start(bf16[1,16,128,80]{2,3,1,0:T(8,128)(2,1)} %param.23) | copy-start | bytes 983044
  88.3 14.5 %copy-start.11 = (bf16[1,16,128,80]{2,3,1,0:T(8,128)(2,1)S(1)}, bf16[1,16,128,80]{2,3,1,0:T(8,128)(2,1)}, u32[]{:S(2)}) copy-start(bf16[1,16,128,80]{2,3,1,0:T(8,128)(2,1)} %param.24) | copy-start | bytes 983044
  88.3 60.4 %all-to-all-start.1 = ((f32[32,1,16,2,4,80]{5,2,4,3,1,0:T(8,128)}), f32[32,1,16,2,4,80]{5,2,4,3,1,0:T(8,128)}, u32[]{:S(2)}, u32[]{:S(2)}) async-start(f32[32,1,16,2,4,80]{5,2,4,3,1,0:T(8,128)} %fusion.11), calls=%async_computation.1 | async-start | bytes 4194304 | tf_op jit(solution)/shard_map/all_to_all | solution.py:69
  98.4 129.3 %all-reduce.3.cloned.1.call-start = ((), (), s32[]{:S(2)}) async-start(), calls=%async_computation.3 | async-start | bytes 327680 | tf_op jit(solution)/shard_map/psum | solution.py:123
  99.0 51.7 %copy-start.13 = (bf16[32,80]{1,0:T(8,128)(2,1)S(1)}, bf16[32,80]{1,0:T(8,128)(2,1)}, u32[]{:S(2)}) copy-start(bf16[32,80]{1,0:T(8,128)(2,1)} %param.20) | copy-start | bytes 15364
  150.6 77.1 %copy-start.2 = (bf16[32,2560]{1,0:T(8,128)(2,1)S(1)}, bf16[32,2560]{1,0:T(8,128)(2,1)}, u32[]{:S(2)}) copy-start(bf16[32,2560]{1,0:T(8,128)(2,1)} %param.17) | copy-start | bytes 491524
  150.6 78.2 %copy-start.6 = (f32[2560]{0:T(1024)S(1)}, f32[2560]{0:T(1024)}, u32[]{:S(2)}) copy-start(f32[2560]{0:T(1024)} %param.31) | copy-start | bytes 30724
  153.5 159.4 %all-reduce.5.cloned.1.call-start = ((), (), s32[]{:S(2)}) async-start(), calls=%async_computation.4 | async-start | bytes 327680 | tf_op jit(solution)/shard_map/psum | solution.py:132
  227.7 3.6 %copy-start.3 = (bf16[32,2560]{1,0:T(8,128)(2,1)S(1)}, bf16[32,2560]{1,0:T(8,128)(2,1)}, u32[]{:S(2)}) copy-start(bf16[32,2560]{1,0:T(8,128)(2,1)} %all-reduce.3.cloned.1.call-done) | copy-start | bytes 491524
  231.3 83.4 %copy-start.7 = (f32[2560]{0:T(1024)S(1)}, f32[2560]{0:T(1024)}, u32[]{:S(2)}) copy-start(f32[2560]{0:T(1024)} %param.33) | copy-start | bytes 30724
  231.3 83.4 %copy-start.8 = (f32[2560]{0:T(1024)S(1)}, f32[2560]{0:T(1024)}, u32[]{:S(2)}) copy-start(f32[2560]{0:T(1024)} %param.32) | copy-start | bytes 30724
Sparse Core Ops, SparseCore 0:
  153.7 73.9 all-reduce.2
  235.8 77.0 all-reduce.4
where the time goes:
time: 323 us; the launch traced here: 322 us
  waiting for transfers between devices  203 us (63%)
  blocking collectives  43.4 us (13%)
  starting transfers between devices  24.9 us (8%)
  matrix products  20.6 us (6%)
  between operations  14.4 us (4%)
  other arithmetic  9.26 us (3%)
  local copies, waits for them, and re-layouts  6.46 us (2%)
    psum x1, waiting for transfers between devices, on_device(): lax.psum(jnp.dot(hidden, down_weight, preferred_element_type=jnp.float32)...  77.2 us
    psum x1, waiting for transfers between devices, on_device(): lax.psum(projected.astype(jnp.bfloat16), 'mlp').astype(jnp.float32)  74.1 us
    all_to_all x1, waiting for transfers between devices, on_device(): lax.all_to_all(piece_out, 'req', split_axis=0, concat_axis=0, tiled=True)  45.6 us
    all_gather x1, blocking collectives, on_device(): gathered = lax.all_gather(queries, 'req', axis=0, tiled=True)  43.4 us
    all_to_all x1, starting transfers between devices, on_device(): lax.all_to_all(piece_out, 'req', split_axis=0, concat_axis=0, tiled=True)  10.1 us
    all_to_all x1, starting transfers between devices, on_device(): lax.all_to_all(piece_sum, 'req', split_axis=0, concat_axis=0, tiled=True)  8.41 us
    dot_general x1, matrix products, on_device(): jnp.einsum('pksjgl,plkh->pksjgh', piece_w.astype(jnp.bfloat16), prefix_va...  7.23 us
  transfers between devices with their start and end apart: 5, of which 4 were waited for; matrix products, arithmetic and copies ran while one was open for 4% of the time, Pallas kernels for 0%

commit v1 on v0

--- a/solution.py
+++ b/solution.py
@@ -120,9 +120,9 @@
     mlp_count = lax.axis_size("mlp")
     mlp_index = lax.axis_index("mlp")
     share = D // mlp_count
-    mid = residual_in.astype(jnp.float32) + lax.psum(projected.astype(jnp.bfloat16), "mlp").astype(
-        jnp.float32
-    )
+    mid = residual_in.astype(jnp.float32) + jnp.sum(
+        lax.all_gather(projected.astype(jnp.bfloat16), "mlp"), axis=0
+    ).astype(jnp.float32)
     normed = (mid * rms_scale(jnp.sum(mid * mid, -1, keepdims=True), D) * mlp_gain).astype(
         jnp.bfloat16
     )

time: 323 us -> 288 us (0.89)
  waiting for transfers between devices: 203 us -> 168 us
    psum x1 -> x0, waiting for transfers between devices: 74.1 us -> none  [on_device(): lax.psum(projected.astype(jnp.bfloat16), 'mlp').astype(jnp.float32)]
    all_gather x0 -> x1, waiting for transfers between devices: none -> 39.1 us  [on_device(): lax.all_gather(projected.astype(jnp.bfloat16), 'mlp')]
where the time goes in v1:
time: 288 us; the launch traced here: 287 us
  waiting for transfers between devices  168 us (58%)
  blocking collectives  43.4 us (15%)
  starting transfers between devices  24.9 us (9%)
  matrix products  20.5 us (7%)
  between operations  14.3 us (5%)
  other arithmetic  9.8 us (3%)
  local copies, waits for them, and re-layouts  6.45 us (2%)
    psum x1, waiting for transfers between devices, on_device(): lax.psum(jnp.dot(hidden, down_weight, preferred_element_type=jnp.float32)...  76.8 us
    all_to_all x1, waiting for transfers between devices, on_device(): lax.all_to_all(piece_out, 'req', split_axis=0, concat_axis=0, tiled=True)  45.6 us
    all_gather x1, blocking collectives, on_device(): gathered = lax.all_gather(queries, 'req', axis=0, tiled=True)  43.4 us
    all_gather x1, waiting for transfers between devices, on_device(): lax.all_gather(projected.astype(jnp.bfloat16), 'mlp')  39.1 us
    all_to_all x1, starting transfers between devices, on_device(): lax.all_to_all(piece_out, 'req', split_axis=0, concat_axis=0, tiled=True)  10.1 us
    all_to_all x1, starting transfers between devices, on_device(): lax.all_to_all(piece_sum, 'req', split_axis=0, concat_axis=0, tiled=True)  8.41 us
    dot_general x1, matrix products, on_device(): jnp.einsum('pksjgl,plkh->pksjgh', piece_w.astype(jnp.bfloat16), prefix_va...  7.23 us
    all_to_all x1, waiting for transfers between devices, on_device(): lax.all_to_all(piece_sum, 'req', split_axis=0, concat_axis=0, tiled=True)  6.39 us
  transfers between devices with their start and end apart: 5, of which 4 were waited for; matrix products, arithmetic and copies ran while one was open for 4% of the time, Pallas kernels for 0%

profile of v1, /device:TPU:6, one launch (start us, length us, event | category | flops | bytes accessed | tf_op | source)
XLA Modules:
  0.0 287.3 jit_solution(8403934674151467521)
XLA Ops:
  7.2 0.0 copy-start
  7.2 0.0 copy-start.8
  7.2 43.4 %all_gather.9 = bf16[1024,320]{1,0:T(8,128)(2,1)S(1)} all-gather(bf16[32,320]{1,0:T(8,128)(2,1)} %param.18), channel_id=1, replica_groups=mesh['req'=32,'mlp'=8] {'req'}, dimensions={0}, use_global_device_ids=true | all-gather | bytes 675840 | tf_op jit(solution)/shard_map/all_gather | solution.py:45
  50.6 1.6 reshape.254
  52.3 0.0 copy-done.8
  52.3 0.1 broadcast_compare_fusion
  52.4 2.8 select_reduce_fusion
  55.2 0.0 copy-start.1
  55.2 2.3 fusion
  57.4 0.9 copy-done.1
  58.4 0.7 reshape.269
  59.1 8.4 %all-to-all-start.2 = ((f32[32,1,128]{2,1,0:T(1,128)}), f32[32,1,128]{2,1,0:T(1,128)S(1)}, u32[]{:S(2)}, u32[]{:S(2)}) async-start(f32[32,1,128]{2,1,0:T(1,128)} %reshape.269), calls=%async_computation.2 | async-start | bytes 32768 | tf_op jit(solution)/shard_map/all_to_all | solution.py:71
  67.6 0.7 reshape.267
  68.3 6.4 %all-to-all-done.2 = f32[32,1,128]{2,1,0:T(1,128)S(1)} async-done(((f32[32,1,128]{2,1,0:T(1,128)}), f32[32,1,128]{2,1,0:T(1,128)S(1)}, u32[]{:S(2)}, u32[]{:S(2)}) %all-to-all-start.2) | async-done | bytes 16416 | tf_op jit(solution)/shard_map/all_to_all | solution.py:71
  74.7 6.3 %all-to-all-start = ((f32[32,1,128]{2,1,0:T(1,128)}), f32[32,1,128]{2,1,0:T(1,128)S(1)}, u32[]{:S(2)}, u32[]{:S(2)}) async-start(f32[32,1,128]{2,1,0:T(1,128)} %reshape.267), calls=%async_computation | async-start | bytes 32768 | tf_op jit(solution)/shard_map/all_to_all | solution.py:70
  81.0 7.2 %fusion.11 = f32[32,1,16,2,4,80]{5,2,4,3,1,0:T(8,128)} fusion(bf16[32,512,80]{1,2,0:T(8,128)(2,1)} %param.22, f32[32,16,2,4,512]{4,1,3,2,0:T(8,128)} %copy-done.1, f32[32,16,2,4]{1,3,2,0:T(4,128)S(1)} %get-tuple-element.8, pred[32,512]{1,0:T(8,128)(4,1)S(1)} %broadcast_compare_fusion), kind=kOutput, calls=%fused_computation.15 | convolution fusion | flops 343932928 | bytes 12353536 | tf_op jit(solution)/shard_map/pksjgl,plkh->pksjgh/dot_general | solution.py:62
  88.3 0.0 copy-start.10
  88.3 0.0 all-to-all-done
  88.3 10.1 %all-to-all-start.1 = ((f32[32,1,16,2,4,80]{5,2,4,3,1,0:T(8,128)}), f32[32,1,16,2,4,80]{5,2,4,3,1,0:T(8,128)}, u32[]{:S(2)}, u32[]{:S(2)}) async-start(f32[32,1,16,2,4,80]{5,2,4,3,1,0:T(8,128)} %fusion.11), calls=%async_computation.1 | async-start | bytes 4194304 | tf_op jit(solution)/shard_map/all_to_all | solution.py:69
  98.4 0.0 all-gather.3.cloned.1.call-start
  98.4 0.1 reshape.255
  98.5 0.0 copy-done.11
  98.5 0.4 select_reduce_fusion.2
  99.0 0.0 copy-start.12
  99.0 0.1 copy.35
  99.1 0.1 iota_compare_fusion
  99.2 0.3 select_reduce_fusion.1
  99.4 0.1 copy.34
  99.5 0.5 broadcast.104
  100.1 0.7 reduce.16
  100.7 0.1 reshape.268
  100.9 0.1 bitcast_reduce_fusion.2
  100.9 0.1 copy.39
  101.0 0.1 fusion.39
  101.2 0.1 copy.44
  101.3 0.2 fusion.31
  101.5 0.1 copy.43
  101.6 0.7 reduce.17
  102.3 0.1 reshape.270
  102.4 0.1 bitcast_reduce_fusion.1
  102.5 0.1 copy.45
  102.6 0.1 copy.38
  102.8 0.3 fusion.22
  103.1 45.6 %all-to-all-done.1 = f32[32,1,16,2,4,80]{5,2,4,3,1,0:T(8,128)} async-done(((f32[32,1,16,2,4,80]{5,2,4,3,1,0:T(8,128)}), f32[32,1,16,2,4,80]{5,2,4,3,1,0:T(8,128)}, u32[]{:S(2)}, u32[]{:S(2)}) %all-to-all-start.1) | async-done | bytes 1310752 | tf_op jit(solution)/shard_map/all_to_all | solution.py:69
  148.7 1.9 bitcast_reduce_fusion
  150.6 0.0 copy-start.2
  150.6 0.0 copy-start.5
  150.6 0.3 fusion.19
  150.9 0.1 reshape_transpose.3
  151.0 2.5 convolution_convert_fusion.1
  153.5 0.0 all-gather.3.cloned.1.call-update
  153.6 0.0 all-reduce.2.cloned.1.call-start
  153.6 39.1 %all-gather.3.cloned.1.call-done = bf16[256,2560]{1,0:T(8,128)(2,1)} async-done(((bf16[32,2560]{1,0:T(8,128)(2,1)}), bf16[256,2560]{1,0:T(8,128)(2,1)}) %all-gather.3.cloned.1.call-update) | async-done | bytes 1310736 | tf_op jit(solution)/shard_map/all_gather | solution.py:124
  192.7 1.5 reduce_sum.92
  194.2 0.2 multiply_reduce_fusion.2
  194.4 2.3 fusion.45
  196.8 0.0 copy-start.7
  196.8 4.3 %convolution_convert_fusion = bf16[32,2560]{1,0:T(8,128)(2,1)} fusion(bf16[512,2560]{1,0:T(8,128)(2,1)} %param.30, bf16[2560,512]{1,0:T(8,128)(2,1)} %param.29, f32[32,512]{1,0:T(8,128)S(1)} %fusion.45, bf16[32,2560]{1,0:T(8,128)(2,1)S(1)} %reduce_sum.92, bf16[32,2560]{1,0:T(8,128)(2,1)S(1)} %copy-done.2, f32[2560]{0:T(1024)S(1)} %copy-done.5, ...), kind=kOutput, calls=%fused_computation.9 | convolution fusion | flops 168443904 | bytes 5810304 | tf_op jit(solution)/shard_map/dot_general | solution.py:133
  201.1 0.0 all-reduce.2.cloned.1.call-update
  201.1 76.8 %all-reduce.2.cloned.1.call-done = bf16[32,2560]{1,0:T(8,128)(2,1)} async-done(((bf16[32,2560]{1,0:T(8,128)(2,1)}), bf16[32,2560]{1,0:T(8,128)(2,1)}) %all-reduce.2.cloned.1.call-update) | async-done | bytes 163856 | tf_op jit(solution)/shard_map/psum | solution.py:132
  277.9 1.1 multiply_reduce_fusion.1
  279.1 0.7 dynamic-slice_convert_fusion
  279.7 0.0 copy-done.6
  279.8 0.7 multiply_reduce_fusion
  (23 shorter events, 0.1 us)
Async XLA Ops:
  7.2 45.2 %copy-start = (bf16[32,512,80]{1,2,0:T(8,128)(2,1)S(1)}, bf16[32,512,80]{1,2,0:T(8,128)(2,1)}, u32[]{:S(2)}) copy-start(bf16[32,512,80]{1,2,0:T(8,128)(2,1)} %param.21) | copy-start | bytes 7864324
  7.2 45.1 %copy-start.8 = (s32[32]{0:T(128)S(1)}, s32[32]{0:T(128)}, u32[]{:S(2)}) copy-start(s32[32]{0:T(128)} %param.25) | copy-start | bytes 388
  55.2 3.2 %copy-start.1 = (f32[32,16,2,4,512]{4,1,3,2,0:T(8,128)}, f32[32,16,2,4,512]{4,1,3,2,0:T(8,128)S(1)}, u32[]{:S(2)}) copy-start(f32[32,16,2,4,512]{4,1,3,2,0:T(8,128)S(1)} %get-tuple-element.9) | copy-start | bytes 25165828
  59.1 15.6 %all-to-all-start.2 = ((f32[32,1,128]{2,1,0:T(1,128)}), f32[32,1,128]{2,1,0:T(1,128)S(1)}, u32[]{:S(2)}, u32[]{:S(2)}) async-start(f32[32,1,128]{2,1,0:T(1,128)} %reshape.269), calls=%async_computation.2 | async-start | bytes 32768 | tf_op jit(solution)/shard_map/all_to_all | solution.py:71
  74.7 13.6 %all-to-all-start = ((f32[32,1,128]{2,1,0:T(1,128)}), f32[32,1,128]{2,1,0:T(1,128)S(1)}, u32[]{:S(2)}, u32[]{:S(2)}) async-start(f32[32,1,128]{2,1,0:T(1,128)} %reshape.267), calls=%async_computation | async-start | bytes 32768 | tf_op jit(solution)/shard_map/all_to_all | solution.py:70
  88.3 10.2 %copy-start.4 = (bf16[32,320]{1,0:T(8,128)(2,1)S(1)}, bf16[32,320]{1,0:T(8,128)(2,1)}, u32[]{:S(2)}) copy-start(bf16[32,320]{1,0:T(8,128)(2,1)} %param.18) | copy-start | bytes 61444
  88.3 10.3 %copy-start.11 = (bf16[32,80]{1,0:T(8,128)(2,1)S(1)}, bf16[32,80]{1,0:T(8,128)(2,1)}, u32[]{:S(2)}) copy-start(bf16[32,80]{1,0:T(8,128)(2,1)} %param.19) | copy-start | bytes 15364
  88.3 10.8 %copy-start.9 = (s32[1,16]{1,0:T(1,128)S(1)}, s32[1,16]{1,0:T(1,128)}, u32[]{:S(2)}) copy-start(s32[1,16]{1,0:T(1,128)} %param.26) | copy-start | bytes 196
  88.3 10.9 %copy-start.3 = (bf16[1,16,128,80]{2,3,1,0:T(8,128)(2,1)S(1)}, bf16[1,16,128,80]{2,3,1,0:T(8,128)(2,1)}, u32[]{:S(2)}) copy-start(bf16[1,16,128,80]{2,3,1,0:T(8,128)(2,1)} %param.23) | copy-start | bytes 983044
  88.3 14.5 %copy-start.10 = (bf16[1,16,128,80]{2,3,1,0:T(8,128)(2,1)S(1)}, bf16[1,16,128,80]{2,3,1,0:T(8,128)(2,1)}, u32[]{:S(2)}) copy-start(bf16[1,16,128,80]{2,3,1,0:T(8,128)(2,1)} %param.24) | copy-start | bytes 983044
  88.3 60.4 %all-to-all-start.1 = ((f32[32,1,16,2,4,80]{5,2,4,3,1,0:T(8,128)}), f32[32,1,16,2,4,80]{5,2,4,3,1,0:T(8,128)}, u32[]{:S(2)}, u32[]{:S(2)}) async-start(f32[32,1,16,2,4,80]{5,2,4,3,1,0:T(8,128)} %fusion.11), calls=%async_computation.1 | async-start | bytes 4194304 | tf_op jit(solution)/shard_map/all_to_all | solution.py:69
  98.4 94.3 %all-gather.3.cloned.1.call-start = ((), (), s32[]{:S(2)}) async-start(), calls=%async_computation.4 | async-start | bytes 1474560 | tf_op jit(solution)/shard_map/all_gather | solution.py:124
  99.0 51.6 %copy-start.12 = (bf16[32,80]{1,0:T(8,128)(2,1)S(1)}, bf16[32,80]{1,0:T(8,128)(2,1)}, u32[]{:S(2)}) copy-start(bf16[32,80]{1,0:T(8,128)(2,1)} %param.20) | copy-start | bytes 15364
  150.6 43.6 %copy-start.2 = (bf16[32,2560]{1,0:T(8,128)(2,1)S(1)}, bf16[32,2560]{1,0:T(8,128)(2,1)}, u32[]{:S(2)}) copy-start(bf16[32,2560]{1,0:T(8,128)(2,1)} %param.17) | copy-start | bytes 491524
  150.6 43.8 %copy-start.5 = (f32[2560]{0:T(1024)S(1)}, f32[2560]{0:T(1024)}, u32[]{:S(2)}) copy-start(f32[2560]{0:T(1024)} %param.31) | copy-start | bytes 30724
  153.6 124.4 %all-reduce.2.cloned.1.call-start = ((), (), s32[]{:S(2)}) async-start(), calls=%async_computation.3 | async-start | bytes 327680 | tf_op jit(solution)/shard_map/psum | solution.py:132
  196.8 83.0 %copy-start.6 = (f32[2560]{0:T(1024)S(1)}, f32[2560]{0:T(1024)}, u32[]{:S(2)}) copy-start(f32[2560]{0:T(1024)} %param.33) | copy-start | bytes 30724
  196.8 83.0 %copy-start.7 = (f32[2560]{0:T(1024)S(1)}, f32[2560]{0:T(1024)}, u32[]{:S(2)}) copy-start(f32[2560]{0:T(1024)} %param.32) | copy-start | bytes 30724
Sparse Core Ops, SparseCore 0:
  153.7 38.9 all-gather.2
  201.2 76.6 all-reduce.1
